TPU v7x, 512 devices: a whole 4x8x8 slice. The times are simulated.
512 devices in a mesh: sub: 128 (over z, y, core), harm: 4 (over x).
Axes of the slice: x: 4, y: 8, z: 8, core: 2. Of those that a mesh axis runs over, the one named last changes fastest.
Arguments:
- lengths: int32 [384], P('sub'), may hold values from 128 to 1024, as said below
- owners: int32 [384, 1], P('sub'), may hold values from 0 to 127, as said below
- front_inverse: bfloat16 [384, 1024, 1024], P('sub', 'harm'), may hold values from -0.1875 to 0.1875
- coupling: bfloat16 [384, 1024, 768], P('sub', 'harm'), may hold values from -0.1875 to 0.1875
- stiffness: bfloat16 [384, 768, 768], P('sub', 'harm'), may hold values from -0.21875 to 0.21875
- displacement: bfloat16 [128, 32, 768], P('sub', 'harm'), may hold values from -6 to 6
- forcing: float32 [128, 32, 768], P('sub', 'harm'), may hold values from -6 to 6
- lumped_mass: float32 [128, 768], P('sub'), may hold values from 0.2 to 2
- damping: float32 [128, 768], P('sub'), may hold values from 0.1 to 1.5
Outputs:
- interior: bfloat16 [384, 32, 1024], P('sub', None, 'harm')
- residual: float32 [128, 32, 768], P('sub', 'harm')
- modes: bfloat16 [384, 1024, 768], P('sub', 'harm')
Inputs may be any that keep to these rules, and one draw needn't show every extreme that they name: `lengths`: live interior front rows of each substructure, which are its first rows; some substructure has all 1024. `owners`: substructure k lies on sub index k // 3; on every sub index d, the first 2 of its 3 substructures are attached to block (d + 64) mod 128, the third to a block of uneven popularity; every interface block has at least one substructure.
All inputs are finite; a program needn't handle non-finite values.
Results may differ from a plain program's by a relative error of at most 0.008.
Values may be sent and summed in bfloat16 or wider, within the bound.
No kernel may reach another device: no remote copies, remote signals or barrier semaphores. Data moves between devices by JAX's collectives and lax.ppermute only.
A program may use at most 64 MiB of HBM per device.

v0:
```python
import jax
import jax.numpy as jnp
from jax import lax
from jax.sharding import PartitionSpec as P


def shifted(x, axis, step):
    n = lax.axis_size(axis)
    return lax.ppermute(x, axis, [(j, (j + step) % n) for j in range(n)])


def column_block(x, index, width):
    return lax.dynamic_slice_in_dim(x, index * width, width, axis=x.ndim - 1)


def body(
    lengths, owners, front_inverse, coupling, stiffness, displacement, forcing, lumped_mass, damping
):
    nharm = lax.axis_size("harm")
    harm_idx = lax.axis_index("harm")
    nsub = lax.axis_size("sub")
    front_q = coupling.shape[1]
    width = coupling.shape[2]
    width_q = stiffness.shape[1]
    rows_q = displacement.shape[1]
    own_rows = harm_idx * front_q + jnp.arange(front_q, dtype=jnp.int32)
    live_rows = own_rows[None, :] < lengths[:, None]
    masked = jnp.where(live_rows[:, :, None], coupling, jnp.zeros_like(coupling))
    from_left = shifted(masked, "harm", 1)
    from_right = shifted(masked, "harm", -1)
    half = front_q // 2
    far = jnp.concatenate(
        [shifted(from_left[:, :half], "harm", 1), shifted(from_right[:, half:], "harm", -1)], axis=1
    )

    def modes_term(block, step):
        cols = column_block(front_inverse, (harm_idx + step) % nharm, front_q)
        return jnp.einsum("sfg,sgn->sfn", cols, block, preferred_element_type=jnp.float32)

    modes = modes_term(masked, 0)
    modes = modes + modes_term(from_left, -1)
    modes = modes + modes_term(from_right, 1)
    modes = (modes + modes_term(far, 2)).astype(jnp.bfloat16)
    disp_rows = displacement[0]
    near_block = shifted(disp_rows, "sub", nsub // 2)
    every_block = lax.all_gather(disp_rows, "sub")
    third_block = lax.dynamic_index_in_dim(every_block, owners[2, 0], 0, keepdims=False)
    picked = jnp.stack([near_block, third_block])
    own_pair = lax.all_gather(picked, "harm", axis=1, tiled=True)
    own_disp = jnp.stack([own_pair[0], own_pair[0], own_pair[1]])
    partial_y = jnp.einsum("shn,sfn->shf", own_disp, masked, preferred_element_type=jnp.float32)
    whole_y = lax.all_gather(partial_y, "harm", axis=2, tiled=True)
    inner = -jnp.einsum(
        "shg,sfg->shf",
        whole_y,
        front_inverse.astype(jnp.float32),
        precision=lax.Precision.HIGHEST,
        preferred_element_type=jnp.float32,
    )
    interior = jnp.where(live_rows[:, None, :], inner, jnp.float32(0.0)).astype(jnp.bfloat16)
    disp_cols = column_block(own_disp, harm_idx, width_q)
    contrib = jnp.einsum("shf,sfn->shn", interior, masked, preferred_element_type=jnp.float32)
    contrib = contrib + jnp.einsum(
        "shj,sjn->shn", disp_cols, stiffness, preferred_element_type=jnp.float32
    )
    pair_sum = jnp.stack([contrib[0] + contrib[1], contrib[2]])
    pair_rows = lax.psum_scatter(pair_sum, "harm", scatter_dimension=1, tiled=True)
    near_sum = shifted(pair_rows[0], "sub", nsub // 2)
    slots = jnp.arange(nsub, dtype=jnp.int32)[:, None, None] == owners[2, 0]
    spread = jnp.where(slots, pair_rows[1][None], jnp.float32(0.0))
    far_sum = lax.psum_scatter(spread, "sub", scatter_dimension=0, tiled=True)
    gathered = near_sum[None] + far_sum
    pairs_all = rows_q * nharm // 2
    rows = harm_idx * rows_q + jnp.arange(rows_q, dtype=jnp.int32)
    pair = (rows // 2).astype(jnp.float32)
    parity = (rows % 2).astype(jnp.float32)
    freq = 1.5 * (pair + 1.0) / pairs_all
    sign = 1.0 - 2.0 * parity
    disp = displacement.astype(jnp.float32)
    partner = disp.reshape(1, rows_q // 2, 2, width)[:, :, ::-1, :].reshape(1, rows_q, width)
    residual = (
        gathered
        - (freq * freq)[None, :, None] * lumped_mass[:, None, :] * disp
        + (sign * freq)[None, :, None] * damping[:, None, :] * partner
        - forcing
    )
    return (interior, residual, modes)


def solution(mesh):
    placed = (
        P("sub"),
        P("sub", None),
        P("sub", "harm", None),
        P("sub", "harm", None),
        P("sub", "harm", None),
        P("sub", "harm", None),
        P("sub", "harm", None),
        P("sub", None),
        P("sub", None),
    )
    return jax.shard_map(
        body,
        mesh=mesh,
        in_specs=placed,
        out_specs=(P("sub", None, "harm"), P("sub", "harm", None), P("sub", "harm", None)),
        check_vma=False,
    )
```

profile of v0, /device:TPU:2, one launch (start us, length us, event | category | flops | bytes accessed | tf_op | source)
XLA Modules:
  0.0 363.1 jit_solution(845991593042576625)
XLA Ops:
  7.2 0.7 all-gather.2.cloned.1.call-update
  8.0 10.9 %collective-permute-start = (bf16[8,768]{1,0:T(8,128)(2,1)}, bf16[8,768]{1,0:T(8,128)(2,1)S(1)}, u32[]{:S(2)}, u32[]{:S(2)}) collective-permute-start(bf16[8,768]{1,0:T(8,128)(2,1)} %bitcast.24), channel_id=1, source_target_pairs={{0,256},{4,260},{8,264},{12,268},{16,272},{20,276},{24,280},{28,28... | collective-permute-start | bytes 36872 | tf_op jit(solution)/shard_map/ppermute | solution.py:9
  18.9 1.2 slice.31
  22.1 0.7 broadcast_compare_fusion
  22.8 1.4 broadcast_select_fusion.1
  24.3 74.2 %all-gather.2.cloned.1.call-done = bf16[128,8,768]{2,1,0:T(8,128)(2,1)} async-done(((bf16[1,8,768]{2,1,0:T(8,128)(2,1)}), bf16[128,8,768]{2,1,0:T(8,128)(2,1)}) %all-gather.2.cloned.1.call-update) | async-done | bytes 1572880 | tf_op jit(solution)/shard_map/all_gather | solution.py:46
  98.4 0.7 constant_dynamic-slice_fusion
  99.2 12.0 %all_gather.10 = bf16[2,32,768]{2,1,0:T(8,128)(2,1)S(1)} all-gather(bf16[2,8,768]{2,1,0:T(8,128)(2,1)S(1)} %pad_maximum_fusion.3), channel_id=1, replica_groups=mesh['sub'=128,'harm'=4] {'harm'}, dimensions={1}, use_global_device_ids=true | all-gather | bytes 122880 | tf_op jit(solution)/shard_map/all_gather | solution.py:49
  111.2 0.5 fusion.15
  111.7 12.5 %all_gather.11 = f32[3,32,1024]{2,1,0:T(8,128)S(1)} all-gather(f32[3,32,256]{2,1,0:T(8,128)S(1)} %fusion.15), channel_id=1, replica_groups=mesh['sub'=128,'harm'=4] {'harm'}, dimensions={2}, use_global_device_ids=true | all-gather | bytes 491520 | tf_op jit(solution)/shard_map/all_gather | solution.py:52
  124.2 1.5 fusion.7
  125.7 0.3 fusion.34
  126.0 0.4 convolution_add_fusion
  126.4 0.7 pad_maximum_fusion
  127.2 0.7 iota_compare_fusion
  127.8 20.8 %reduce-scatter.3.cloned.1.call-done = f32[2,8,768]{2,1,0:T(8,128)} async-done(((f32[2,32,768]{2,1,0:T(8,128)}), f32[2,8,768]{2,1,0:T(8,128)}) %reduce-scatter.3.cloned.1.call-update) | async-done | bytes 49168 | tf_op jit(solution)/shard_map/reduce_scatter | solution.py:67
  148.6 0.8 slice_bitcast_fusion.1
  149.4 1.9 broadcast_select_fusion
  151.3 3.7 %collective-permute-start.3 = (bf16[3,256,768]{2,1,0:T(8,128)(2,1)S(1)}, bf16[3,256,768]{2,1,0:T(8,128)(2,1)}, u32[]{:S(2)}, u32[]{:S(2)}) collective-permute-start(bf16[3,256,768]{2,1,0:T(8,128)(2,1)S(1)} %broadcast_select_fusion.1), channel_id=1, source_target_pairs={{0,3},{1,0},{2,1},{3,2},{4,7},{5,4},{6,5},{7,6},{8,11},{9,8},{10,9... | collective-permute-start | bytes 3538952 | tf_op jit(solution)/shard_map/ppermute | solution.py:9
  155.1 2.2 collective-permute-start.2
  157.8 0.5 fusion.13
  158.3 20.2 %collective-permute-done.3 = bf16[3,256,768]{2,1,0:T(8,128)(2,1)} collective-permute-done((bf16[3,256,768]{2,1,0:T(8,128)(2,1)S(1)}, bf16[3,256,768]{2,1,0:T(8,128)(2,1)}, u32[]{:S(2)}, u32[]{:S(2)}) %collective-permute-start.3) | collective-permute-done | bytes 1179680 | tf_op jit(solution)/shard_map/ppermute | solution.py:9
  178.4 1.1 slice.47
  179.5 4.1 %collective-permute-start.5 = (bf16[3,128,768]{2,1,0:T(8,128)(2,1)S(1)}, bf16[3,128,768]{2,1,0:T(8,128)(2,1)S(1)}, u32[]{:S(2)}, u32[]{:S(2)}) collective-permute-start(bf16[3,128,768]{2,1,0:T(8,128)(2,1)S(1)} %slice.47), channel_id=1, source_target_pairs={{0,3},{1,0},{2,1},{3,2},{4,7},{5,4},{6,5},{7,6},{8,11},{9,8},{10,9... | collective-permute-start | bytes 1769480 | tf_op jit(solution)/shard_map/ppermute | solution.py:9
  183.6 1.1 slice.46
  184.8 1.9 collective-permute-start.4
  186.7 1.8 fusion.9
  188.5 1.8 fusion.11
  190.2 8.1 %collective-permute-start.1 = (f32[8,768]{1,0:T(8,128)S(1)}, f32[8,768]{1,0:T(8,128)S(1)}, u32[]{:S(2)}, u32[]{:S(2)}) collective-permute-start(f32[8,768]{1,0:T(8,128)S(1)} %get-tuple-element.5), channel_id=1, source_target_pairs={{0,256},{4,260},{8,264},{12,268},{16,272},{20,276},{24,280},{28,28... | collective-permute-start | bytes 73736 | tf_op jit(solution)/shard_map/ppermute | solution.py:9
  198.4 1.7 add_convert_fusion
  200.1 155.0 %reduce-scatter.5.cloned.1.call-done = f32[1,8,768]{2,1,0:T(8,128)} async-done(((f32[128,8,768]{2,1,0:T(8,128)}), f32[1,8,768]{2,1,0:T(8,128)}) %reduce-scatter.5.cloned.1.call-update) | async-done | bytes 24592 | tf_op jit(solution)/shard_map/reduce_scatter | solution.py:71
  355.1 1.4 fusion.20
  (34 shorter events, 0.7 us)
Async XLA Ops:
  7.2 117.1 %copy-start = (bf16[3,256,1024]{2,1,0:T(8,128)(2,1)S(1)}, bf16[3,256,1024]{2,1,0:T(8,128)(2,1)}, u32[]{:S(2)}) copy-start(bf16[3,256,1024]{2,1,0:T(8,128)(2,1)} %param.11) | copy-start | bytes 4718596
  7.2 91.3 %all-gather.2.cloned.1.call-start = ((), (), s32[]{:S(2)}) async-start(), calls=%async_computation.2 | async-start | bytes 1585152 | tf_op jit(solution)/shard_map/all_gather | solution.py:46
  7.9 140.7 %reduce-scatter.3.cloned.1.call-start = ((), (), s32[]{:S(2)}) async-start(), calls=%async_computation.3 | async-start | bytes 245760 | tf_op jit(solution)/shard_map/reduce_scatter | solution.py:67
  8.0 91.2 %collective-permute-start = (bf16[8,768]{1,0:T(8,128)(2,1)}, bf16[8,768]{1,0:T(8,128)(2,1)S(1)}, u32[]{:S(2)}, u32[]{:S(2)}) collective-permute-start(bf16[8,768]{1,0:T(8,128)(2,1)} %bitcast.24), channel_id=1, source_target_pairs={{0,256},{4,260},{8,264},{12,268},{16,272},{20,276},{24,280},{28,28... | collective-permute-start | bytes 36872 | tf_op jit(solution)/shard_map/ppermute | solution.py:9
  124.2 1.8 copy-start.1
  125.7 0.7 copy-start.2
  127.1 228.0 %reduce-scatter.5.cloned.1.call-start = ((), (), s32[]{:S(2)}) async-start(), calls=%async_computation.4 | async-start | bytes 3170304 | tf_op jit(solution)/shard_map/reduce_scatter | solution.py:71
  151.3 6.1 %copy-start.3 = (bf16[1,8,768]{2,1,0:T(8,128)(2,1)S(1)}, bf16[1,8,768]{2,1,0:T(8,128)(2,1)}, u32[]{:S(2)}) copy-start(bf16[1,8,768]{2,1,0:T(8,128)(2,1)} %param.14) | copy-start | bytes 36868
  151.3 6.1 %copy-start.5 = (f32[1,768]{1,0:T(1,128)S(1)}, f32[1,768]{1,0:T(1,128)}, u32[]{:S(2)}) copy-start(f32[1,768]{1,0:T(1,128)} %param.16) | copy-start | bytes 9220
  151.3 6.2 %copy-start.6 = (f32[1,768]{1,0:T(1,128)S(1)}, f32[1,768]{1,0:T(1,128)}, u32[]{:S(2)}) copy-start(f32[1,768]{1,0:T(1,128)} %param.17) | copy-start | bytes 9220
  151.3 27.1 %collective-permute-start.3 = (bf16[3,256,768]{2,1,0:T(8,128)(2,1)S(1)}, bf16[3,256,768]{2,1,0:T(8,128)(2,1)}, u32[]{:S(2)}, u32[]{:S(2)}) collective-permute-start(bf16[3,256,768]{2,1,0:T(8,128)(2,1)S(1)} %broadcast_select_fusion.1), channel_id=1, source_target_pairs={{0,3},{1,0},{2,1},{3,2},{4,7},{5,4},{6,5},{7,6},{8,11},{9,8},{10,9... | collective-permute-start | bytes 3538952 | tf_op jit(solution)/shard_map/ppermute | solution.py:9
  155.1 28.6 %collective-permute-start.2 = (bf16[3,256,768]{2,1,0:T(8,128)(2,1)S(1)}, bf16[3,256,768]{2,1,0:T(8,128)(2,1)}, u32[]{:S(2)}, u32[]{:S(2)}) collective-permute-start(bf16[3,256,768]{2,1,0:T(8,128)(2,1)S(1)} %broadcast_select_fusion.1), channel_id=1, source_target_pairs={{0,1},{1,2},{2,3},{3,0},{4,5},{5,6},{6,7},{7,4},{8,9},{9,10},{10,1... | collective-permute-start | bytes 3538952 | tf_op jit(solution)/shard_map/ppermute | solution.py:9
  179.5 18.8 %collective-permute-start.5 = (bf16[3,128,768]{2,1,0:T(8,128)(2,1)S(1)}, bf16[3,128,768]{2,1,0:T(8,128)(2,1)S(1)}, u32[]{:S(2)}, u32[]{:S(2)}) collective-permute-start(bf16[3,128,768]{2,1,0:T(8,128)(2,1)S(1)} %slice.47), channel_id=1, source_target_pairs={{0,3},{1,0},{2,1},{3,2},{4,7},{5,4},{6,5},{7,6},{8,11},{9,8},{10,9... | collective-permute-start | bytes 1769480 | tf_op jit(solution)/shard_map/ppermute | solution.py:9
  184.8 13.6 %collective-permute-start.4 = (bf16[3,128,768]{2,1,0:T(8,128)(2,1)S(1)}, bf16[3,128,768]{2,1,0:T(8,128)(2,1)S(1)}, u32[]{:S(2)}, u32[]{:S(2)}) collective-permute-start(bf16[3,128,768]{2,1,0:T(8,128)(2,1)S(1)} %slice.46), channel_id=1, source_target_pairs={{0,1},{1,2},{2,3},{3,0},{4,5},{5,6},{6,7},{7,4},{8,9},{9,10},{10,1... | collective-permute-start | bytes 1769480 | tf_op jit(solution)/shard_map/ppermute | solution.py:9
  190.2 164.9 %copy-start.4 = (f32[1,8,768]{2,1,0:T(8,128)S(1)}, f32[1,8,768]{2,1,0:T(8,128)}, u32[]{:S(2)}) copy-start(f32[1,8,768]{2,1,0:T(8,128)} %param.15) | copy-start | bytes 73732
  190.2 9.9 %collective-permute-start.1 = (f32[8,768]{1,0:T(8,128)S(1)}, f32[8,768]{1,0:T(8,128)S(1)}, u32[]{:S(2)}, u32[]{:S(2)}) collective-permute-start(f32[8,768]{1,0:T(8,128)S(1)} %get-tuple-element.5), channel_id=1, source_target_pairs={{0,256},{4,260},{8,264},{12,268},{16,272},{20,276},{24,280},{28,28... | collective-permute-start | bytes 73736 | tf_op jit(solution)/shard_map/ppermute | solution.py:9
Sparse Core Ops, SparseCore 0:
  11.2 87.1 all-gather.1
  127.2 21.3 reduce-scatter.2
  153.6 201.4 reduce-scatter.4
where the time goes:
time: 364 us; the launch traced here: 363 us
  waiting for transfers between devices  271 us (74%)
  starting transfers between devices  31.1 us (9%)
  blocking collectives  24.6 us (7%)
  between operations  16 us (4%)
  matrix products  8.27 us (2%)
  other arithmetic  6.92 us (2%)
  local copies, waits for them, and re-layouts  5.23 us (1%)
    reduce_scatter x1, waiting for transfers between devices, body(): far_sum = lax.psum_scatter(spread, 'sub', scatter_dimension=0, tiled=True)  155 us
    all_gather x1, waiting for transfers between devices, body(): every_block = lax.all_gather(disp_rows, 'sub')  74.2 us
    ppermute x6, starting transfers between devices, shifted(): return lax.ppermute(x, axis, [(j, (j + step) % n) for j in range(n)])  31 us
    reduce_scatter x1, waiting for transfers between devices, body(): lax.psum_scatter(pair_sum, 'harm', scatter_dimension=1, tiled=True)  20.8 us
    ppermute x6, waiting for transfers between devices, shifted(): return lax.ppermute(x, axis, [(j, (j + step) % n) for j in range(n)])  20.3 us
    all_gather x1, blocking collectives, body(): whole_y = lax.all_gather(partial_y, 'harm', axis=2, tiled=True)  12.5 us
    all_gather x1, blocking collectives, body(): own_pair = lax.all_gather(picked, 'harm', axis=1, tiled=True)  12 us
  transfers between devices with their start and end apart: 9, of which 5 were waited for; matrix products, arithmetic and copies ran while one was open for 4% of the time, Pallas kernels for 0%

commit v1 on v0

--- a/solution.py
+++ b/solution.py
@@ -46,7 +46,12 @@
     every_block = lax.all_gather(disp_rows, "sub")
     third_block = lax.dynamic_index_in_dim(every_block, owners[2, 0], 0, keepdims=False)
     picked = jnp.stack([near_block, third_block])
-    own_pair = lax.all_gather(picked, "harm", axis=1, tiled=True)
+    ring = [picked]
+    for hop in range(3):
+        ring.append(lax.ppermute(ring[-1], "harm", [(dev, (dev + 1) % 4) for dev in range(4)]))
+    own_pair = jnp.roll(
+        jnp.concatenate(ring[::-1], axis=1), (lax.axis_index("harm") + 1) * ring[0].shape[1], axis=1
+    )
     own_disp = jnp.stack([own_pair[0], own_pair[0], own_pair[1]])
     partial_y = jnp.einsum("shn,sfn->shf", own_disp, masked, preferred_element_type=jnp.float32)
     whole_y = lax.all_gather(partial_y, "harm", axis=2, tiled=True)

time: 364 us -> 372 us (1.022)
  blocking collectives: 24.6 us -> 12.9 us
  starting transfers between devices: 31.1 us -> 41.2 us
  waiting for transfers between devices: 271 us -> 280 us
    all_gather x1 -> x0, blocking collectives: 12 us -> none  [body(): own_pair = lax.all_gather(picked, 'harm', axis=1, tiled=True)]
    ppermute x0 -> x3, starting transfers between devices: none -> 10.1 us  [body(): lax.ppermute(ring[-1], 'harm', [(dev, (dev + 1) % 4) for dev in range(4)])]
    ppermute x0 -> x3, waiting for transfers between devices: none -> 5.76 us  [body(): lax.ppermute(ring[-1], 'harm', [(dev, (dev + 1) % 4) for dev in range(4)])]
  transfers between devices with their start and end apart: 9 -> 12, of which waited for: 5 -> 8; matrix products, arithmetic and copies ran while one was open for 4% -> 3% of each run, Pallas kernels for 0% -> 0%
where the time goes in v1:
time: 372 us; the launch traced here: 371 us
  waiting for transfers between devices  280 us (75%)
  starting transfers between devices  41.2 us (11%)
  between operations  16.1 us (4%)
  blocking collectives  12.9 us (3%)
  matrix products  8.25 us (2%)
  other arithmetic  6.95 us (2%)
  local copies, waits for them, and re-layouts  5.28 us (1%)
    reduce_scatter x1, waiting for transfers between devices, body(): far_sum = lax.psum_scatter(spread, 'sub', scatter_dimension=0, tiled=True)  155 us
    all_gather x1, waiting for transfers between devices, body(): every_block = lax.all_gather(disp_rows, 'sub')  76.4 us
    ppermute x6, starting transfers between devices, shifted(): return lax.ppermute(x, axis, [(j, (j + step) % n) for j in range(n)])  31 us
    reduce_scatter x1, waiting for transfers between devices, body(): lax.psum_scatter(pair_sum, 'harm', scatter_dimension=1, tiled=True)  21.9 us
    ppermute x6, waiting for transfers between devices, shifted(): return lax.ppermute(x, axis, [(j, (j + step) % n) for j in range(n)])  20.3 us
    all_gather x1, blocking collectives, body(): whole_y = lax.all_gather(partial_y, 'harm', axis=2, tiled=True)  12.9 us
    ppermute x3, starting transfers between devices, body(): lax.ppermute(ring[-1], 'harm', [(dev, (dev + 1) % 4) for dev in range(4)])  10.1 us
  transfers between devices with their start and end apart: 12, of which 8 were waited for; matrix products, arithmetic and copies ran while one was open for 3% of the time, Pallas kernels for 0%

profile of v1, /device:TPU:2, one launch (start us, length us, event | category | flops | bytes accessed | tf_op | source)
XLA Modules:
  0.0 370.7 jit_solution(12259081377761028249)
XLA Ops:
  7.2 0.7 all-gather.2.cloned.1.call-update
  8.0 10.9 %collective-permute-start = (bf16[8,768]{1,0:T(8,128)(2,1)}, bf16[8,768]{1,0:T(8,128)(2,1)S(1)}, u32[]{:S(2)}, u32[]{:S(2)}) collective-permute-start(bf16[8,768]{1,0:T(8,128)(2,1)} %bitcast.24), channel_id=1, source_target_pairs={{0,256},{4,260},{8,264},{12,268},{16,272},{20,276},{24,280},{28,28... | collective-permute-start | bytes 36872 | tf_op jit(solution)/shard_map/ppermute | solution.py:9
  18.9 1.2 slice.31
  22.1 76.4 %all-gather.2.cloned.1.call-done = bf16[128,8,768]{2,1,0:T(8,128)(2,1)} async-done(((bf16[1,8,768]{2,1,0:T(8,128)(2,1)}), bf16[128,8,768]{2,1,0:T(8,128)(2,1)}) %all-gather.2.cloned.1.call-update) | async-done | bytes 1572880 | tf_op jit(solution)/shard_map/all_gather | solution.py:46
  98.4 0.7 constant_dynamic-slice_fusion.2
  99.2 3.4 collective-permute-start.1
  102.6 2.3 collective-permute-done.1
  104.9 3.4 collective-permute-start.2
  108.3 0.7 broadcast_compare_fusion
  109.0 1.6 collective-permute-done.2
  110.6 3.4 collective-permute-start.3
  114.0 1.4 broadcast_select_fusion.1
  115.4 1.8 collective-permute-done.3
  117.9 12.9 %all_gather.7 = f32[3,32,1024]{2,1,0:T(8,128)S(1)} all-gather(f32[3,32,256]{2,1,0:T(8,128)S(1)} %fusion.15), channel_id=1, replica_groups=mesh['sub'=128,'harm'=4] {'harm'}, dimensions={2}, use_global_device_ids=true | all-gather | bytes 491520 | tf_op jit(solution)/shard_map/all_gather | solution.py:57
  130.8 1.4 fusion.7
  133.0 0.7 pad_maximum_fusion
  134.4 21.9 %reduce-scatter.3.cloned.1.call-done = f32[2,8,768]{2,1,0:T(8,128)} async-done(((f32[2,32,768]{2,1,0:T(8,128)}), f32[2,8,768]{2,1,0:T(8,128)}) %reduce-scatter.3.cloned.1.call-update) | async-done | bytes 49168 | tf_op jit(solution)/shard_map/reduce_scatter | solution.py:72
  156.3 0.8 slice_bitcast_fusion.1
  157.0 1.9 broadcast_select_fusion
  159.0 3.7 collective-permute-start.6
  162.7 2.3 collective-permute-start.5
  165.9 20.2 %collective-permute-done.6 = bf16[3,256,768]{2,1,0:T(8,128)(2,1)} collective-permute-done((bf16[3,256,768]{2,1,0:T(8,128)(2,1)S(1)}, bf16[3,256,768]{2,1,0:T(8,128)(2,1)}, u32[]{:S(2)}, u32[]{:S(2)}) %collective-permute-start.6) | collective-permute-done | bytes 1179680 | tf_op jit(solution)/shard_map/ppermute | solution.py:9
  186.1 1.1 slice.46
  187.2 4.1 %collective-permute-start.8 = (bf16[3,128,768]{2,1,0:T(8,128)(2,1)S(1)}, bf16[3,128,768]{2,1,0:T(8,128)(2,1)S(1)}, u32[]{:S(2)}, u32[]{:S(2)}) collective-permute-start(bf16[3,128,768]{2,1,0:T(8,128)(2,1)S(1)} %slice.46), channel_id=1, source_target_pairs={{0,3},{1,0},{2,1},{3,2},{4,7},{5,4},{6,5},{7,6},{8,11},{9,8},{10,9... | collective-permute-start | bytes 1769480 | tf_op jit(solution)/shard_map/ppermute | solution.py:9
  191.3 1.1 slice.45
  192.4 1.9 collective-permute-start.7
  194.3 1.8 fusion.9
  196.1 1.8 fusion.11
  197.9 8.1 %collective-permute-start.4 = (f32[8,768]{1,0:T(8,128)S(1)}, f32[8,768]{1,0:T(8,128)S(1)}, u32[]{:S(2)}, u32[]{:S(2)}) collective-permute-start(f32[8,768]{1,0:T(8,128)S(1)} %get-tuple-element.5), channel_id=1, source_target_pairs={{0,256},{4,260},{8,264},{12,268},{16,272},{20,276},{24,280},{28,28... | collective-permute-start | bytes 73736 | tf_op jit(solution)/shard_map/ppermute | solution.py:9
  206.0 1.6 add_convert_fusion
  207.8 155.0 %reduce-scatter.5.cloned.1.call-done = f32[1,8,768]{2,1,0:T(8,128)} async-done(((f32[128,8,768]{2,1,0:T(8,128)}), f32[1,8,768]{2,1,0:T(8,128)}) %reduce-scatter.5.cloned.1.call-update) | async-done | bytes 24592 | tf_op jit(solution)/shard_map/reduce_scatter | solution.py:76
  362.8 1.4 fusion.20
  (48 shorter events, 3.0 us)
Async XLA Ops:
  7.2 123.6 %copy-start = (bf16[3,256,1024]{2,1,0:T(8,128)(2,1)S(1)}, bf16[3,256,1024]{2,1,0:T(8,128)(2,1)}, u32[]{:S(2)}) copy-start(bf16[3,256,1024]{2,1,0:T(8,128)(2,1)} %param.11) | copy-start | bytes 4718596
  7.2 91.3 %all-gather.2.cloned.1.call-start = ((), (), s32[]{:S(2)}) async-start(), calls=%async_computation.2 | async-start | bytes 1585152 | tf_op jit(solution)/shard_map/all_gather | solution.py:46
  7.9 148.3 %reduce-scatter.3.cloned.1.call-start = ((), (), s32[]{:S(2)}) async-start(), calls=%async_computation.3 | async-start | bytes 245760 | tf_op jit(solution)/shard_map/reduce_scatter | solution.py:72
  8.0 91.2 %collective-permute-start = (bf16[8,768]{1,0:T(8,128)(2,1)}, bf16[8,768]{1,0:T(8,128)(2,1)S(1)}, u32[]{:S(2)}, u32[]{:S(2)}) collective-permute-start(bf16[8,768]{1,0:T(8,128)(2,1)} %bitcast.24), channel_id=1, source_target_pairs={{0,256},{4,260},{8,264},{12,268},{16,272},{20,276},{24,280},{28,28... | collective-permute-start | bytes 36872 | tf_op jit(solution)/shard_map/ppermute | solution.py:9
  99.2 5.7 %collective-permute-start.1 = (bf16[2,8,768]{2,1,0:T(8,128)(2,1)S(1)}, bf16[2,8,768]{2,1,0:T(8,128)(2,1)S(1)}, u32[]{:S(2)}, u32[]{:S(2)}) collective-permute-start(bf16[2,8,768]{2,1,0:T(8,128)(2,1)S(1)} %pad_maximum_fusion.3), channel_id=1, source_target_pairs={{0,1},{1,2},{2,3},{3,0},{4,5},{5,6},{6,7},{7,4},{8,9},{9,10},{10,1... | collective-permute-start | bytes 73736 | tf_op jit(solution)/shard_map/ppermute | solution.py:51
  104.9 5.7 %collective-permute-start.2 = (bf16[2,8,768]{2,1,0:T(8,128)(2,1)S(1)}, bf16[2,8,768]{2,1,0:T(8,128)(2,1)S(1)}, u32[]{:S(2)}, u32[]{:S(2)}) collective-permute-start(bf16[2,8,768]{2,1,0:T(8,128)(2,1)S(1)} %collective-permute-done.1), channel_id=1, source_target_pairs={{0,1},{1,2},{2,3},{3,0},{4,5},{5,6},{6,7},{7,4},{8,9},{9,10},{10,1... | collective-permute-start | bytes 73736 | tf_op jit(solution)/shard_map/ppermute | solution.py:51
  110.6 6.7 %collective-permute-start.3 = (bf16[2,8,768]{2,1,0:T(8,128)(2,1)S(1)}, bf16[2,8,768]{2,1,0:T(8,128)(2,1)S(1)}, u32[]{:S(2)}, u32[]{:S(2)}) collective-permute-start(bf16[2,8,768]{2,1,0:T(8,128)(2,1)S(1)} %collective-permute-done.2), channel_id=1, source_target_pairs={{0,1},{1,2},{2,3},{3,0},{4,5},{5,6},{6,7},{7,4},{8,9},{9,10},{10,1... | collective-permute-start | bytes 73736 | tf_op jit(solution)/shard_map/ppermute | solution.py:51
  130.8 1.8 copy-start.1
  132.2 0.7 copy-start.2
  133.7 229.1 %reduce-scatter.5.cloned.1.call-start = ((), (), s32[]{:S(2)}) async-start(), calls=%async_computation.4 | async-start | bytes 3170304 | tf_op jit(solution)/shard_map/reduce_scatter | solution.py:76
  158.9 6.1 %copy-start.3 = (bf16[1,8,768]{2,1,0:T(8,128)(2,1)S(1)}, bf16[1,8,768]{2,1,0:T(8,128)(2,1)}, u32[]{:S(2)}) copy-start(bf16[1,8,768]{2,1,0:T(8,128)(2,1)} %param.14) | copy-start | bytes 36868
  159.0 6.1 %copy-start.5 = (f32[1,768]{1,0:T(1,128)S(1)}, f32[1,768]{1,0:T(1,128)}, u32[]{:S(2)}) copy-start(f32[1,768]{1,0:T(1,128)} %param.16) | copy-start | bytes 9220
  159.0 6.1 %copy-start.6 = (f32[1,768]{1,0:T(1,128)S(1)}, f32[1,768]{1,0:T(1,128)}, u32[]{:S(2)}) copy-start(f32[1,768]{1,0:T(1,128)} %param.17) | copy-start | bytes 9220
  159.0 27.1 %collective-permute-start.6 = (bf16[3,256,768]{2,1,0:T(8,128)(2,1)S(1)}, bf16[3,256,768]{2,1,0:T(8,128)(2,1)}, u32[]{:S(2)}, u32[]{:S(2)}) collective-permute-start(bf16[3,256,768]{2,1,0:T(8,128)(2,1)S(1)} %broadcast_select_fusion.1), channel_id=1, source_target_pairs={{0,3},{1,0},{2,1},{3,2},{4,7},{5,4},{6,5},{7,6},{8,11},{9,8},{10,9... | collective-permute-start | bytes 3538952 | tf_op jit(solution)/shard_map/ppermute | solution.py:9
  162.7 28.6 %collective-permute-start.5 = (bf16[3,256,768]{2,1,0:T(8,128)(2,1)S(1)}, bf16[3,256,768]{2,1,0:T(8,128)(2,1)}, u32[]{:S(2)}, u32[]{:S(2)}) collective-permute-start(bf16[3,256,768]{2,1,0:T(8,128)(2,1)S(1)} %broadcast_select_fusion.1), channel_id=1, source_target_pairs={{0,1},{1,2},{2,3},{3,0},{4,5},{5,6},{6,7},{7,4},{8,9},{9,10},{10,1... | collective-permute-start | bytes 3538952 | tf_op jit(solution)/shard_map/ppermute | solution.py:9
  187.2 18.8 %collective-permute-start.8 = (bf16[3,128,768]{2,1,0:T(8,128)(2,1)S(1)}, bf16[3,128,768]{2,1,0:T(8,128)(2,1)S(1)}, u32[]{:S(2)}, u32[]{:S(2)}) collective-permute-start(bf16[3,128,768]{2,1,0:T(8,128)(2,1)S(1)} %slice.46), channel_id=1, source_target_pairs={{0,3},{1,0},{2,1},{3,2},{4,7},{5,4},{6,5},{7,6},{8,11},{9,8},{10,9... | collective-permute-start | bytes 1769480 | tf_op jit(solution)/shard_map/ppermute | solution.py:9
  192.4 13.6 %collective-permute-start.7 = (bf16[3,128,768]{2,1,0:T(8,128)(2,1)S(1)}, bf16[3,128,768]{2,1,0:T(8,128)(2,1)S(1)}, u32[]{:S(2)}, u32[]{:S(2)}) collective-permute-start(bf16[3,128,768]{2,1,0:T(8,128)(2,1)S(1)} %slice.45), channel_id=1, source_target_pairs={{0,1},{1,2},{2,3},{3,0},{4,5},{5,6},{6,7},{7,4},{8,9},{9,10},{10,1... | collective-permute-start | bytes 1769480 | tf_op jit(solution)/shard_map/ppermute | solution.py:9
  197.9 164.9 %copy-start.4 = (f32[1,8,768]{2,1,0:T(8,128)S(1)}, f32[1,8,768]{2,1,0:T(8,128)}, u32[]{:S(2)}) copy-start(f32[1,8,768]{2,1,0:T(8,128)} %param.15) | copy-start | bytes 73732
  197.9 9.9 %collective-permute-start.4 = (f32[8,768]{1,0:T(8,128)S(1)}, f32[8,768]{1,0:T(8,128)S(1)}, u32[]{:S(2)}, u32[]{:S(2)}) collective-permute-start(f32[8,768]{1,0:T(8,128)S(1)} %get-tuple-element.5), channel_id=1, source_target_pairs={{0,256},{4,260},{8,264},{12,268},{16,272},{20,276},{24,280},{28,28... | collective-permute-start | bytes 73736 | tf_op jit(solution)/shard_map/ppermute | solution.py:9
Sparse Core Ops, SparseCore 0:
  11.2 87.1 all-gather.1
  133.8 22.4 reduce-scatter.2
  161.3 201.4 reduce-scatter.4
